TPU v7x, 512 devices: a whole 4x4x16 slice. The times are simulated.
512 devices in a mesh: replica: 64 (over z, x), shard: 8 (over y, core).
Axes of the slice: x: 4, y: 4, z: 16, core: 2. Of those that a mesh axis runs over, the one named last changes fastest.
Arguments:
- grad_query: float32 [512, 512, 384], P(('replica', 'shard')), may hold values from -1.25 to 1.25
- grad_output: float32 [512, 384, 512], P(('replica', 'shard')), may hold values from -1.25 to 1.25
- grad_norm: float32 [512, 512], P(('replica', 'shard')), may hold values from -1.25 to 1.25
- grad_bias: float32 [512, 32, 6], P(('replica', 'shard')), may hold values from -0.3 to 0.3
- weight_query: float32 [512, 384], P('shard'), may hold values from -5.303301 to 5.303301
- weight_output: float32 [384, 512], P('shard'), may hold values from -6.1237244 to 6.1237244
- weight_norm: float32 [512], P('shard'), may hold values from 0 to 120
- weight_bias: float32 [32, 6], P('shard'), may hold values from -120 to 120
- first_query: float32 [512, 384], P('shard'), may hold values from -120 to 120
- first_output: float32 [384, 512], P('shard'), may hold values from -120 to 120
- first_norm: float32 [512], P('shard'), may hold values from -120 to 120
- first_bias: float32 [32, 6], P('shard'), may hold values from -120 to 120
- second_query: float32 [512, 384], P('shard'), may hold values from 0.05 to 2
- second_output: float32 [384, 512], P('shard'), may hold values from 0.05 to 2
- second_norm: float32 [512], P('shard'), may hold values from 0.05 to 2
- second_bias: float32 [32, 6], P('shard'), may hold values from 0.05 to 2
Outputs:
- updated_query: bfloat16 [512, 384], replicated
- updated_output: bfloat16 [384, 512], replicated
- updated_norm: bfloat16 [512], replicated
- updated_bias: bfloat16 [32, 6], replicated
- first_query_next: float32 [512, 384], P('shard')
- first_output_next: float32 [384, 512], P('shard')
- first_norm_next: float32 [512], P('shard')
- first_bias_next: float32 [32, 6], P('shard')
- second_query_next: float32 [512, 384], P('shard')
- second_output_next: float32 [384, 512], P('shard')
- second_norm_next: float32 [512], P('shard')
- second_bias_next: float32 [32, 6], P('shard')
- norm_table: float32 [2, 4], replicated
- trust_ratios: float32 [4], replicated
All inputs are finite; a program needn't handle non-finite values.
Results may differ from a plain program's by a relative error of at most 0.008.
Values may be sent and summed in bfloat16 or wider, within the bound.
No kernel may reach another device: no remote copies, remote signals or barrier semaphores. Data moves between devices by JAX's collectives and lax.ppermute only.
A program may use at most 64 MiB of HBM per device.

v0:
```python
import jax
import jax.numpy as jnp
from jax import lax
from jax.sharding import PartitionSpec as P


def step_math(summed, moment, second, weight, decay_rate):
    moment_next = 0.5 * moment + 0.5 * summed
    second_next = 0.5 * second + 0.5 * summed * summed
    update = moment_next / (jnp.sqrt(second_next) + 1e-06) + decay_rate * weight
    return (moment_next, second_next, update)


def on_device(
    grad_query,
    grad_output,
    grad_norm,
    grad_bias,
    weight_query,
    weight_output,
    weight_norm,
    weight_bias,
    first_query,
    first_output,
    first_norm,
    first_bias,
    second_query,
    second_output,
    second_norm,
    second_bias,
):
    weights = (weight_query, weight_output, weight_norm, weight_bias)
    moments = (first_query, first_output, first_norm, first_bias)
    seconds = (second_query, second_output, second_norm, second_bias)
    decay_rates = (0.01, 0.01, 0.0, 0.0)
    gradients = (grad_query[0], grad_output[0], grad_norm[0], grad_bias[0])
    totals = lax.psum(
        (gradients[0], gradients[1], gradients[2], gradients[3]), ("replica", "shard")
    )
    position = lax.axis_index("shard")
    summed_all = tuple(
        (
            lax.dynamic_slice_in_dim(entire, position * weight.shape[0], weight.shape[0], 0)
            for entire, weight in zip(totals, weights)
        )
    )
    results = [
        step_math(
            summed_all[member],
            moments[member],
            seconds[member],
            weights[member],
            decay_rates[member],
        )
        for member in range(4)
    ]
    weight_squares = [jnp.sum(weight * weight) for weight in weights]
    update_squares = [jnp.sum(result[2] * result[2]) for result in results]
    couples = [
        lax.psum((weight_squares[member], update_squares[member]), "shard") for member in range(4)
    ]
    weight_sizes = jnp.sqrt(jnp.stack([couple[0] for couple in couples]))
    update_sizes = jnp.sqrt(jnp.stack([couple[1] for couple in couples]))
    trust_ratios = weight_sizes / (update_sizes + 1e-06)
    shards = tuple(
        (
            (weights[member] - 0.01 * trust_ratios[member] * results[member][2]).astype(
                jnp.bfloat16
            )
            for member in range(4)
        )
    )
    gathered = (
        lax.all_gather(shards[0], "shard", axis=0, tiled=True),
        lax.all_gather(shards[1], "shard", axis=0, tiled=True),
        lax.all_gather(shards[2], "shard", axis=0, tiled=True),
        lax.all_gather(shards[3], "shard", axis=0, tiled=True),
    )
    norm_table = jnp.stack([weight_sizes, update_sizes])
    return (
        gathered[0],
        gathered[1],
        gathered[2],
        gathered[3],
        results[0][0],
        results[1][0],
        results[2][0],
        results[3][0],
        results[0][1],
        results[1][1],
        results[2][1],
        results[3][1],
        norm_table,
        trust_ratios,
    )


def solution(mesh):
    placed = (
        P(("replica", "shard"), None, None),
        P(("replica", "shard"), None, None),
        P(("replica", "shard"), None),
        P(("replica", "shard"), None, None),
        P("shard", None),
        P("shard", None),
        P("shard"),
        P("shard", None),
        P("shard", None),
        P("shard", None),
        P("shard"),
        P("shard", None),
        P("shard", None),
        P("shard", None),
        P("shard"),
        P("shard", None),
    )
    return jax.shard_map(
        on_device,
        mesh=mesh,
        in_specs=placed,
        out_specs=(
            P(),
            P(),
            P(),
            P(),
            P("shard", None),
            P("shard", None),
            P("shard"),
            P("shard", None),
            P("shard", None),
            P("shard", None),
            P("shard"),
            P("shard", None),
            P(),
            P(),
        ),
        check_vma=False,
    )
```

profile of v0, /device:TPU:1, one launch (start us, length us, event | category | flops | bytes accessed | tf_op | source)
XLA Modules:
  0.0 580.5 jit_solution(12802664677548248440)
XLA Ops:
  7.2 0.0 all-reduce.6.cloned.1.call-start
  7.2 0.0 copy-start.12
  7.2 0.0 copy-start.13
  7.2 0.0 copy-start.14
  7.3 0.0 copy-start.17
  7.3 0.6 all-reduce.6.cloned.1.call-update
  7.9 0.1 copy.32
  8.0 1.3 dynamic-slice
  10.0 111.8 %all-reduce.1 = (f32[32,6]{1,0:T(8,128)S(1)}, f32[512]{0:T(512)S(1)}) all-reduce(f32[32,6]{1,0:T(8,128)S(1)} %bitcast.30, f32[512]{0:T(512)S(1)} %bitcast.32), channel_id=1, replica_groups=mesh['replica'=64,'shard'=8] {'replica','shard'}, use_global_device_ids=true, to_apply=%region_17.0 | all-reduce | flops 704 | bytes 5632 | tf_op jit(solution)/shard_map/psum | solution.py:37
  121.8 1.2 multiply_reduce_fusion.6
  123.0 1.2 multiply_reduce_fusion.4
  124.2 366.8 %all-reduce.6.cloned.1.call-done = (f32[384,512]{1,0:T(8,128)}, f32[512,384]{1,0:T(8,128)}) async-done(((f32[384,512]{1,0:T(8,128)}, f32[512,384]{1,0:T(8,128)}), (f32[384,512]{1,0:T(8,128)}, f32[512,384]{1,0:T(8,128)})) %all-reduce.6.cloned.1.call-update) | async-done | bytes 1572880 | tf_op jit(solution)/shard_map/psum | solution.py:37
  491.0 0.0 copy-start.8
  491.0 0.0 copy-start.9
  491.0 1.7 multiply_reduce_fusion.1
  492.7 1.6 multiply_reduce_fusion
  494.4 14.6 %all-reduce.3 = (f32[]{:T(128)}, f32[]{:T(128)}, f32[]{:T(128)}, f32[]{:T(128)}, f32[]{:T(128)}, /*index=5*/f32[]{:T(128)}, f32[]{:T(128)}, f32[]{:T(128)}) all-reduce(f32[]{:T(128)} %get-tuple-element.70, f32[]{:T(128)} %get-tuple-element.75, f32[]{:T(128)} %get-tuple-element.45, ...), channel_id=1, replica_groups=mesh['replica'=64,'shard'=8] {'shard'}, use_global_device_ids=true, to_apply=%region_7.0 | all-reduce | flops 8 | bytes 64 | tf_op jit(solution)/shard_map/psum | solution.py:60
  508.9 5.1 fusion.5
  514.1 0.0 copy-start.10
  514.1 0.6 fusion.11
  515.3 0.1 subtract_convert_fusion.1
  515.4 14.0 %all_gather.12 = bf16[512,384]{1,0:T(8,128)(2,1)S(1)} all-gather(bf16[64,384]{1,0:T(8,128)(2,1)S(1)} %subtract_convert_fusion.1), channel_id=1, replica_groups=mesh['replica'=64,'shard'=8] {'shard'}, dimensions={0}, use_global_device_ids=true | all-gather | bytes 442368 | tf_op jit(solution)/shard_map/all_gather | solution.py:74
  530.0 0.1 subtract_convert_fusion
  530.1 13.0 %all_gather.13 = bf16[384,512]{1,0:T(8,128)(2,1)S(1)} all-gather(bf16[48,512]{1,0:T(8,128)(2,1)S(1)} %subtract_convert_fusion), channel_id=1, replica_groups=mesh['replica'=64,'shard'=8] {'shard'}, dimensions={0}, use_global_device_ids=true | all-gather | bytes 442368 | tf_op jit(solution)/shard_map/all_gather | solution.py:75
  543.7 0.2 dynamic-update-slice
  544.0 12.5 %all-reduce = bf16[512]{0:T(512)(128)(2,1)} all-reduce(bf16[512]{0:T(512)(128)(2,1)S(1)} %dynamic-update-slice), channel_id=1, replica_groups=mesh['replica'=64,'shard'=8] {'shard'}, use_global_device_ids=true, to_apply=%add | all-reduce | flops 512 | bytes 2048
  557.1 8.6 %all-gather = bf16[8,4,6]{2,1,0:T(4,128)(2,1)S(1)} all-gather(bf16[1,4,6]{2,1,0:T(4,128)(2,1)S(1)} %fusion.3), channel_id=1, replica_groups=mesh['replica'=64,'shard'=8] {'shard'}, dimensions={0}, use_global_device_ids=true | all-gather | bytes 432 | tf_op jit(solution)/shard_map/all_gather | solution.py:77
  565.7 0.7 copy.33
  566.4 5.1 maximum_sqrt_fusion.2
  571.5 0.6 pad_maximum_fusion
  572.1 0.7 copy.41
  572.9 0.7 copy.42
  (34 shorter events, 0.1 us)
Async XLA Ops:
  7.2 483.8 %all-reduce.6.cloned.1.call-start = ((), (), s32[]{:S(2)}) async-start(), calls=%async_computation | async-start | bytes 3145728 | tf_op jit(solution)/shard_map/psum | solution.py:37
  7.2 0.7 copy-start.12
  7.2 2.7 copy-start.13
  7.2 114.5 %copy-start.14 = (f32[64]{0:T(128)S(1)}, f32[64]{0:T(128)}, u32[]{:S(2)}) copy-start(f32[64]{0:T(128)} %param.22) | copy-start | bytes 772
  7.3 114.5 %copy-start.17 = (f32[64]{0:T(128)S(1)}, f32[64]{0:T(128)}, u32[]{:S(2)}) copy-start(f32[64]{0:T(128)} %param.30) | copy-start | bytes 772
  7.3 114.5 %copy-start.18 = (f32[64]{0:T(128)S(1)}, f32[64]{0:T(128)}, u32[]{:S(2)}) copy-start(f32[64]{0:T(128)} %param.26) | copy-start | bytes 772
  7.3 115.7 %copy-start.11 = (f32[4,6]{1,0:T(4,128)S(1)}, f32[4,6]{1,0:T(4,128)}, u32[]{:S(2)}) copy-start(f32[4,6]{1,0:T(4,128)} %param.23) | copy-start | bytes 292
  7.3 115.7 %copy-start.15 = (f32[4,6]{1,0:T(4,128)S(1)}, f32[4,6]{1,0:T(4,128)}, u32[]{:S(2)}) copy-start(f32[4,6]{1,0:T(4,128)} %param.31) | copy-start | bytes 292
  7.3 115.7 %copy-start.16 = (f32[4,6]{1,0:T(4,128)S(1)}, f32[4,6]{1,0:T(4,128)}, u32[]{:S(2)}) copy-start(f32[4,6]{1,0:T(4,128)} %param.27) | copy-start | bytes 292
  7.3 483.6 %copy-start.6 = (f32[64,384]{1,0:T(8,128)S(1)}, f32[64,384]{1,0:T(8,128)}, u32[]{:S(2)}) copy-start(f32[64,384]{1,0:T(8,128)} %param.28) | copy-start | bytes 294916
  7.3 483.6 %copy-start.7 = (f32[64,384]{1,0:T(8,128)S(1)}, f32[64,384]{1,0:T(8,128)}, u32[]{:S(2)}) copy-start(f32[64,384]{1,0:T(8,128)} %param.24) | copy-start | bytes 294916
  7.9 483.0 %copy-start = (f32[64,384]{1,0:T(8,128)S(1)}, f32[64,384]{1,0:T(8,128)}, u32[]{:S(2)}) copy-start(f32[64,384]{1,0:T(8,128)} %param.20) | copy-start | bytes 294916
  491.0 1.7 copy-start.1
  491.0 1.7 copy-start.8
  491.0 1.7 copy-start.9
  492.7 22.6 %copy-start.2 = (f32[64,384]{1,0:T(8,128)}, f32[64,384]{1,0:T(8,128)S(1)}, u32[]{:S(2)}) copy-start(f32[64,384]{1,0:T(8,128)S(1)} %get-tuple-element.100) | copy-start | bytes 294916
  492.7 22.6 %copy-start.3 = (f32[64,384]{1,0:T(8,128)}, f32[64,384]{1,0:T(8,128)S(1)}, u32[]{:S(2)}) copy-start(f32[64,384]{1,0:T(8,128)S(1)} %get-tuple-element.96) | copy-start | bytes 294916
  494.4 35.6 %copy-start.4 = (f32[48,512]{1,0:T(8,128)}, f32[48,512]{1,0:T(8,128)S(1)}, u32[]{:S(2)}) copy-start(f32[48,512]{1,0:T(8,128)S(1)} %get-tuple-element.101) | copy-start | bytes 294916
  494.4 35.6 %copy-start.5 = (f32[48,512]{1,0:T(8,128)}, f32[48,512]{1,0:T(8,128)S(1)}, u32[]{:S(2)}) copy-start(f32[48,512]{1,0:T(8,128)S(1)} %get-tuple-element.97) | copy-start | bytes 294916
  514.1 0.6 copy-start.10
Sparse Core Ops, SparseCore 0:
  13.4 477.5 all-reduce.5
where the time goes:
time: 581 us; the launch traced here: 580 us
  waiting for transfers between devices  367 us (63%)
  blocking collectives  174 us (30%)
  between operations  17.4 us (3%)
  other arithmetic  16.7 us (3%)
    psum x1, waiting for transfers between devices, on_device(): lax.psum((gradients[0], gradients[1], gradients[2], gradients[3]), ('repl...  367 us
    psum x1, blocking collectives, on_device(): lax.psum((gradients[0], gradients[1], gradients[2], gradients[3]), ('repl...  112 us
    psum x1, blocking collectives, on_device(): lax.psum((weight_squares[member], update_squares[member]), 'shard')  14.6 us
    all_gather x1, blocking collectives, on_device(): lax.all_gather(shards[0], 'shard', axis=0, tiled=True)  14 us
    all_gather x1, blocking collectives, on_device(): lax.all_gather(shards[1], 'shard', axis=0, tiled=True)  13 us
    unnamed x1, blocking collectives  12.5 us
  transfers between devices with their start and end apart: 1, of which 1 were waited for; matrix products, arithmetic and copies ran while one was open for 1% of the time, Pallas kernels for 0%

commit v1 on v0

--- a/solution.py
+++ b/solution.py
@@ -34,8 +34,12 @@
     seconds = (second_query, second_output, second_norm, second_bias)
     decay_rates = (0.01, 0.01, 0.0, 0.0)
     gradients = (grad_query[0], grad_output[0], grad_norm[0], grad_bias[0])
-    totals = lax.psum(
-        (gradients[0], gradients[1], gradients[2], gradients[3]), ("replica", "shard")
+
+    def enter_stops_all(m, dev_axis, axis_name):
+        return jax.lax.psum(jax.lax.psum(m, axis_name=dev_axis), axis_name=axis_name)
+
+    totals = enter_stops_all(
+        (gradients[0], gradients[1], gradients[2], gradients[3]), "replica", "shard"
     )
     position = lax.axis_index("shard")
     summed_all = tuple(

time: 581 us -> 688 us (1.18)
  blocking collectives: 174 us -> 370 us
  waiting for transfers between devices: 367 us -> 277 us
    psum x1 -> x2, blocking collectives: 112 us -> 307 us  [the longest x1 222 us: enter_stops_all(): jax.lax.psum(m, axis_name=dev_axis)]
    psum x1 -> x2, waiting for transfers between devices: 367 us -> 276 us  [the longest x1 276 us: enter_stops_all(): jax.lax.psum(m, axis_name=dev_axis)]
  transfers between devices with their start and end apart: 1 -> 2, of which waited for: 1 -> 1; matrix products, arithmetic and copies ran while one was open for 1% -> 1% of each run, Pallas kernels for 0% -> 0%
where the time goes in v1:
time: 688 us; the launch traced here: 687 us
  blocking collectives  370 us (54%)
  waiting for transfers between devices  277 us (40%)
  between operations  17.4 us (3%)
  other arithmetic  16.7 us (2%)
    psum x1, waiting for transfers between devices, enter_stops_all(): jax.lax.psum(m, axis_name=dev_axis)  276 us
    psum x1, blocking collectives, enter_stops_all(): jax.lax.psum(m, axis_name=dev_axis)  222 us
    psum x1, blocking collectives, enter_stops_all(): jax.lax.psum(jax.lax.psum(m, axis_name=dev_axis), axis_name=axis_name)  85.2 us
    psum x1, blocking collectives, on_device(): lax.psum((weight_squares[member], update_squares[member]), 'shard')  16 us
  transfers between devices with their start and end apart: 2, of which 1 were waited for; matrix products, arithmetic and copies ran while one was open for 1% of the time, Pallas kernels for 0%

profile of v1, /device:TPU:1, one launch (start us, length us, event | category | flops | bytes accessed | tf_op | source)
XLA Modules:
  0.0 687.5 jit_solution(7431582791191107202)
XLA Ops:
  7.2 0.0 all-reduce.9.cloned.1.call-start
  7.2 0.7 all-reduce.9.cloned.1.call-update
  7.9 0.0 all-reduce.11.cloned.1.call-start
  8.0 276.4 %all-reduce.9.cloned.1.call-done = (f32[384,512]{1,0:T(8,128)}, f32[512,384]{1,0:T(8,128)}) async-done(((f32[384,512]{1,0:T(8,128)}, f32[512,384]{1,0:T(8,128)}), (f32[384,512]{1,0:T(8,128)}, f32[512,384]{1,0:T(8,128)})) %all-reduce.9.cloned.1.call-update) | async-done | bytes 1572880 | tf_op jit(solution)/shard_map/psum | solution.py:39
  284.4 0.0 all-reduce.11.cloned.1.call-update
  284.4 0.6 copy-done.12
  285.1 0.1 copy.32
  285.1 1.3 dynamic-slice
  287.1 0.0 copy-start.11
  287.1 0.0 copy-start.15
  287.1 221.7 %all-reduce.1 = (f32[32,6]{1,0:T(8,128)S(1)}, f32[512]{0:T(512)S(1)}) all-reduce(f32[32,6]{1,0:T(8,128)S(1)} %bitcast.30, f32[512]{0:T(512)S(1)} %bitcast.32), channel_id=1, replica_groups=mesh['replica'=64,'shard'=8] {'replica'}, use_global_device_ids=true, to_apply=%region_20.0 | all-reduce | flops 704 | bytes 5632 | tf_op jit(solution)/shard_map/psum | solution.py:39
  508.8 85.2 %all-reduce.4 = (f32[32,6]{1,0:T(8,128)S(1)}, f32[512]{0:T(512)S(1)}) all-reduce(f32[32,6]{1,0:T(8,128)S(1)} %get-tuple-element.46, f32[512]{0:T(512)S(1)} %get-tuple-element.47), channel_id=1, replica_groups=mesh['replica'=64,'shard'=8] {'shard'}, use_global_device_ids=true, to_apply=%region_21.0 | all-reduce | flops 704 | bytes 5632 | tf_op jit(solution)/shard_map/psum | solution.py:39
  594.0 0.6 copy-done.14
  594.6 1.2 multiply_reduce_fusion.6
  595.8 1.2 multiply_reduce_fusion.4
  597.1 1.7 multiply_reduce_fusion.1
  598.8 1.6 multiply_reduce_fusion
  600.5 16.0 %all-reduce.3 = (f32[]{:T(128)}, f32[]{:T(128)}, f32[]{:T(128)}, f32[]{:T(128)}, f32[]{:T(128)}, /*index=5*/f32[]{:T(128)}, f32[]{:T(128)}, f32[]{:T(128)}) all-reduce(f32[]{:T(128)} %get-tuple-element.74, f32[]{:T(128)} %get-tuple-element.79, f32[]{:T(128)} %get-tuple-element.45, ...), channel_id=1, replica_groups=mesh['replica'=64,'shard'=8] {'shard'}, use_global_device_ids=true, to_apply=%region_7.0 | all-reduce | flops 8 | bytes 64 | tf_op jit(solution)/shard_map/psum | solution.py:64
  616.5 5.1 fusion.5
  621.7 0.6 fusion.11
  622.8 0.1 subtract_convert_fusion.1
  622.9 13.5 %all_gather.12 = bf16[512,384]{1,0:T(8,128)(2,1)S(1)} all-gather(bf16[64,384]{1,0:T(8,128)(2,1)S(1)} %subtract_convert_fusion.1), channel_id=1, replica_groups=mesh['replica'=64,'shard'=8] {'shard'}, dimensions={0}, use_global_device_ids=true | all-gather | bytes 442368 | tf_op jit(solution)/shard_map/all_gather | solution.py:78
  637.0 0.1 subtract_convert_fusion
  637.1 13.0 %all_gather.13 = bf16[384,512]{1,0:T(8,128)(2,1)S(1)} all-gather(bf16[48,512]{1,0:T(8,128)(2,1)S(1)} %subtract_convert_fusion), channel_id=1, replica_groups=mesh['replica'=64,'shard'=8] {'shard'}, dimensions={0}, use_global_device_ids=true | all-gather | bytes 442368 | tf_op jit(solution)/shard_map/all_gather | solution.py:79
  650.7 0.2 dynamic-update-slice
  651.0 12.5 %all-reduce = bf16[512]{0:T(512)(128)(2,1)} all-reduce(bf16[512]{0:T(512)(128)(2,1)S(1)} %dynamic-update-slice), channel_id=1, replica_groups=mesh['replica'=64,'shard'=8] {'shard'}, use_global_device_ids=true, to_apply=%add | all-reduce | flops 512 | bytes 2048
  664.1 8.6 %all-gather = bf16[8,4,6]{2,1,0:T(4,128)(2,1)S(1)} all-gather(bf16[1,4,6]{2,1,0:T(4,128)(2,1)S(1)} %fusion.3), channel_id=1, replica_groups=mesh['replica'=64,'shard'=8] {'shard'}, dimensions={0}, use_global_device_ids=true | all-gather | bytes 432 | tf_op jit(solution)/shard_map/all_gather | solution.py:81
  672.8 0.7 copy.33
  673.4 5.1 maximum_sqrt_fusion.2
  678.6 0.6 pad_maximum_fusion
  679.1 0.7 copy.43
  679.9 0.7 copy.44
  (38 shorter events, 0.1 us)
Async XLA Ops:
  7.2 277.2 %all-reduce.9.cloned.1.call-start = ((), (), s32[]{:S(2)}) async-start(), calls=%async_computation | async-start | bytes 3145728 | tf_op jit(solution)/shard_map/psum | solution.py:39
  7.9 589.1 %all-reduce.11.cloned.1.call-start = ((), (), s32[]{:S(2)}) async-start(), calls=%async_computation.1 | async-start | bytes 3145728 | tf_op jit(solution)/shard_map/psum | solution.py:39
  284.4 0.7 copy-start.12
  284.4 2.7 copy-start.13
  284.4 309.6 %copy-start.17 = (f32[64]{0:T(128)S(1)}, f32[64]{0:T(128)}, u32[]{:S(2)}) copy-start(f32[64]{0:T(128)} %param.30) | copy-start | bytes 772
  284.4 309.6 %copy-start.18 = (f32[64]{0:T(128)S(1)}, f32[64]{0:T(128)}, u32[]{:S(2)}) copy-start(f32[64]{0:T(128)} %param.26) | copy-start | bytes 772
  284.4 312.7 %copy-start.6 = (f32[64,384]{1,0:T(8,128)S(1)}, f32[64,384]{1,0:T(8,128)}, u32[]{:S(2)}) copy-start(f32[64,384]{1,0:T(8,128)} %param.28) | copy-start | bytes 294916
  284.4 312.7 %copy-start.7 = (f32[64,384]{1,0:T(8,128)S(1)}, f32[64,384]{1,0:T(8,128)}, u32[]{:S(2)}) copy-start(f32[64,384]{1,0:T(8,128)} %param.24) | copy-start | bytes 294916
  284.4 312.6 %copy-start = (f32[64,384]{1,0:T(8,128)S(1)}, f32[64,384]{1,0:T(8,128)}, u32[]{:S(2)}) copy-start(f32[64,384]{1,0:T(8,128)} %param.20) | copy-start | bytes 294916
  287.1 308.8 %copy-start.11 = (f32[4,6]{1,0:T(4,128)S(1)}, f32[4,6]{1,0:T(4,128)}, u32[]{:S(2)}) copy-start(f32[4,6]{1,0:T(4,128)} %param.23) | copy-start | bytes 292
  287.1 308.8 %copy-start.15 = (f32[4,6]{1,0:T(4,128)S(1)}, f32[4,6]{1,0:T(4,128)}, u32[]{:S(2)}) copy-start(f32[4,6]{1,0:T(4,128)} %param.31) | copy-start | bytes 292
  287.1 308.8 %copy-start.16 = (f32[4,6]{1,0:T(4,128)S(1)}, f32[4,6]{1,0:T(4,128)}, u32[]{:S(2)}) copy-start(f32[4,6]{1,0:T(4,128)} %param.27) | copy-start | bytes 292
  594.0 0.7 copy-start.14
  597.0 1.8 copy-start.1
  597.1 1.8 copy-start.8
  597.1 1.7 copy-start.9
  598.8 24.0 %copy-start.2 = (f32[64,384]{1,0:T(8,128)}, f32[64,384]{1,0:T(8,128)S(1)}, u32[]{:S(2)}) copy-start(f32[64,384]{1,0:T(8,128)S(1)} %get-tuple-element.104) | copy-start | bytes 294916
  598.8 24.0 %copy-start.3 = (f32[64,384]{1,0:T(8,128)}, f32[64,384]{1,0:T(8,128)S(1)}, u32[]{:S(2)}) copy-start(f32[64,384]{1,0:T(8,128)S(1)} %get-tuple-element.100) | copy-start | bytes 294916
  600.5 36.5 %copy-start.4 = (f32[48,512]{1,0:T(8,128)}, f32[48,512]{1,0:T(8,128)S(1)}, u32[]{:S(2)}) copy-start(f32[48,512]{1,0:T(8,128)S(1)} %get-tuple-element.105) | copy-start | bytes 294916
  600.5 36.5 %copy-start.5 = (f32[48,512]{1,0:T(8,128)}, f32[48,512]{1,0:T(8,128)S(1)}, u32[]{:S(2)}) copy-start(f32[48,512]{1,0:T(8,128)S(1)} %get-tuple-element.101) | copy-start | bytes 294916
  621.6 0.6 copy-start.10
Sparse Core Ops, SparseCore 0:
  11.5 272.8 all-reduce.8
  286.8 82.2 all-reduce.10
